TPU v7x, 256 devices: a whole 4x4x8 slice. The times are simulated.
256 devices in a mesh: cent: 8 (over z), dp: 32 (over x, y, core).
Axes of the slice: x: 4, y: 4, z: 8, core: 2. Of those that a mesh axis runs over, the one named last changes fastest.
Arguments:
- points: bfloat16 [32768, 1024], P('dp'), may hold values from -6 to 6
- cluster_ids: int32 [32768, 1], P('dp'), may hold values from 0 to 63; in each aligned block of 1024 rows (0 to 1023, 1024 to 2047, ...) at most 64 rows name the same one
- centroids: bfloat16 [8192, 1024], P('cent'), may hold values from -6 to 6
- sub_centroids: bfloat16 [64, 1024, 1024], P('dp', 'cent'), may hold values from -6 to 6
Outputs:
- assign: bfloat16 [32768, 8192], P('dp', 'cent')
- sub_assign: bfloat16 [32768, 1024], P('dp', 'cent')
Inputs may be any that keep to these rules, and one draw needn't show every extreme that they name: `cluster_ids`: among the 1024 points of one index of dp, no level-two cluster holds more than 64 points; some cluster holds exactly 64 in some block.
All inputs are finite; a program needn't handle non-finite values.
Results may differ from a plain program's by a relative error of at most 0.001.
Values may be sent and summed in bfloat16 or wider, within the bound.
No kernel may reach another device: no remote copies, remote signals or barrier semaphores. Data moves between devices by JAX's collectives and lax.ppermute only.
A program may use at most 128 MiB of HBM per device.

v0:
```python
import jax
import jax.numpy as jnp
from jax import lax
from jax.sharding import PartitionSpec as P

CAP = 64
ITERS = 3
EPS = 1e-06
TAU = 0.05


def inverse_norm(rows):
    values = rows.astype(jnp.float32)
    return lax.rsqrt(jnp.mean(values * values, axis=-1) + EPS)


def shards(points, cluster_ids, centroids, sub_centroids):
    pts_count = points.shape[0]
    width = points.shape[1]
    dp_count = lax.axis_size("dp")
    cent_count = lax.axis_size("cent")
    group_dev = sub_centroids.shape[0]
    sub_dev = sub_centroids.shape[1]
    clusters = group_dev * dp_count
    total_cent = centroids.shape[0] * cent_count
    total_sub = sub_dev * cent_count
    inv_x = inverse_norm(points)
    inv_c = inverse_norm(centroids)
    inv_u = inverse_norm(sub_centroids)
    scores = jnp.einsum("pd,kd->pk", points, centroids, preferred_element_type=jnp.float32)
    expo = jnp.exp(scores * inv_x[:, None] * inv_c[None, :] * (1.0 / (width * TAU)))
    row_scale = jnp.ones((pts_count,), jnp.float32)
    col_scale = jnp.ones((centroids.shape[0],), jnp.float32)
    row_part = row_scale
    for step in range(ITERS):
        col_part = jnp.dot(row_scale, expo, precision=lax.Precision.HIGHEST)
        col_scale = 1.0 / lax.psum(col_part, "dp")
        row_part = jnp.dot(expo, col_scale, precision=lax.Precision.HIGHEST)
        if step + 1 < ITERS:
            row_scale = 1.0 / lax.psum(row_part, "cent")
    ids = cluster_ids[:, 0]
    labels = lax.broadcasted_iota(jnp.int32, (pts_count, clusters), 1)
    onehot = ids[:, None] == labels
    positions = lax.broadcasted_iota(jnp.int32, (pts_count, pts_count), 0)
    earlier = (positions > positions.T).astype(jnp.bfloat16)
    before = jnp.dot(earlier, onehot.astype(jnp.bfloat16), preferred_element_type=jnp.float32)
    rank = jnp.sum(before * onehot.astype(jnp.float32), axis=1).astype(jnp.int32)
    slot = ids * CAP + rank
    buffer = jnp.zeros((clusters * CAP, width), jnp.bfloat16).at[slot].set(points)
    scale_two = 1.0 / (width * TAU)
    outgoing = buffer.reshape(dp_count, group_dev * CAP, width)
    arrived = lax.all_to_all(outgoing, "dp", split_axis=0, concat_axis=0, tiled=True)
    arrived = arrived.reshape(dp_count, group_dev, CAP, width)
    inv_rows = inverse_norm(arrived)
    dots = jnp.einsum("sgcd,gkd->sgck", arrived, sub_centroids, preferred_element_type=jnp.float32)
    weights = jnp.exp(dots * inv_rows[..., None] * inv_u[None, :, None, :] * scale_two)
    weights = weights.reshape(dp_count, group_dev * CAP, sub_dev)
    returned = lax.all_to_all(weights, "dp", split_axis=0, concat_axis=0, tiled=True)
    slot_weights = returned.reshape(clusters * CAP, sub_dev)
    point_weights = slot_weights[slot]
    denom_part = jnp.sum(point_weights, axis=1)
    row_total = lax.psum(row_part, "cent")
    denominator = lax.psum(denom_part, "cent")
    row_scale = 1.0 / row_total
    assign = (expo * row_scale[:, None] * col_scale[None, :] * total_cent).astype(jnp.bfloat16)
    sub_assign = (total_sub * point_weights / denominator[:, None]).astype(jnp.bfloat16)
    return (assign, sub_assign)


def solution(mesh):
    return jax.shard_map(
        shards,
        mesh=mesh,
        in_specs=(P("dp", None), P("dp", None), P("cent", None), P("dp", "cent", None)),
        out_specs=(P("dp", "cent"), P("dp", "cent")),
        check_vma=False,
    )
```

profile of v0, /device:TPU:0, one launch (start us, length us, event | category | flops | bytes accessed | tf_op | source)
XLA Modules:
  0.0 412.9 jit_solution(17542967821555174308)
XLA Ops:
  0.6 1.4 fusion.11
  2.0 0.7 compare_select_fusion
  2.7 10.8 %scatter_custom_fusion = bf16[4096,1024]{1,0:T(8,128)(2,1)} fusion(s32[1024]{0:T(1024)S(1)} %bitcast.56, bf16[1024,1024]{1,0:T(8,128)(2,1)} %param.4, bf16[]{:T(256)} %constant.6.clone.1), kind=kCustom, calls=%fused_computation.6 | custom fusion | bytes 8389120 | tf_op jit(solution)/shard_map/scatter | solution.py:49
  13.5 0.0 copy-start.1
  13.5 6.1 %all-to-all-start = ((bf16[32,128,1024]{2,1,0:T(8,128)(2,1)}), bf16[32,128,1024]{2,1,0:T(8,128)(2,1)}, u32[]{:S(2)}, u32[]{:S(2)}) async-start(bf16[32,128,1024]{2,1,0:T(8,128)(2,1)} %bitcast.51), calls=%async_computation | async-start | bytes 16777216 | tf_op jit(solution)/shard_map/all_to_all | solution.py:52
  19.6 0.0 copy-start.2
  19.6 2.2 multiply_reduce_fusion.1
  21.8 0.0 copy-done.1
  21.8 0.5 multiply_reduce_fusion.2
  22.3 0.0 copy-done.2
  22.3 2.6 multiply_exponential_fusion
  24.9 0.0 copy-start
  24.9 1.9 copy-done
  26.9 0.0 copy-start.3
  26.9 2.1 fusion.14
  28.9 141.6 %psum.49 = f32[1024]{0:T(1024)S(1)} all-reduce(f32[1024]{0:T(1024)S(1)} %bitcast.55), channel_id=1, replica_groups=mesh['cent'=8,'dp'=32] {'dp'}, use_global_device_ids=true, to_apply=%region_2.0 | all-reduce | flops 1024 | bytes 8192 | tf_op jit(solution)/shard_map/psum | solution.py:37
  170.5 5.8 %fusion.17 = f32[1,1024]{1,0:T(1,128)S(1)} fusion(f32[1024,1024]{1,0:T(8,128)} %copy-done, f32[1024,1]{0,1:T(1,128)S(1)} %bitcast.61), kind=kOutput, calls=%fused_computation.39 | convolution fusion | flops 12582912 | bytes 4202496 | tf_op jit(solution)/shard_map/dot_general | solution.py:38
  176.3 20.0 %psum.50 = f32[1024]{0:T(1024)S(1)} all-reduce(f32[1024]{0:T(1024)S(1)} %bitcast.62), channel_id=1, replica_groups=mesh['cent'=8,'dp'=32] {'cent'}, use_global_device_ids=true, to_apply=%region_3.0 | all-reduce | flops 1024 | bytes 8192 | tf_op jit(solution)/shard_map/psum | solution.py:40
  196.3 0.0 copy-done.3
  196.3 0.2 multiply_reduce_fusion.3
  196.5 0.0 all-to-all-done
  196.5 5.1 %multiply_reduce_fusion = f32[32,128]{1,0:T(8,128)S(1)} fusion(bf16[32,128,1024]{2,1,0:T(8,128)(2,1)} %all-to-all-done), kind=kLoop, calls=%fused_computation.2 | loop fusion | flops 12578816 | bytes 8404992 | tf_op jit(solution)/shard_map/reduce_sum | solution.py:14
  201.6 0.1 rsqrt.34
  201.7 4.8 %fusion.7 = f32[32,2,64,128]{3,2,0,1:T(8,128)S(1)} fusion(bf16[32,2,64,1024]{3,2,1,0:T(8,128)(2,1)} %bitcast.16, f32[2,128]{1,0:T(2,128)S(1)} %add_rsqrt_fusion.3, f32[32,2,64]{2,0,1:T(8,128)S(1)} %copy.7, bf16[2,128,1024]{2,1,0:T(8,128)(2,1)S(1)} %copy-done.3), kind=kOutput, calls=%fused_computation.16 | convolution fusion | flops 1075314688 | bytes 11027456 | tf_op jit(solution)/shard_map/sgcd,gkd->sgck/dot_general | solution.py:55
  206.5 1.5 copy.8
  208.0 5.4 %all-to-all-start.1 = ((f32[32,128,128]{2,1,0:T(8,128)}), f32[32,128,128]{2,1,0:T(8,128)S(1)}, u32[]{:S(2)}, u32[]{:S(2)}) async-start(f32[32,128,128]{2,1,0:T(8,128)} %bitcast.53), calls=%async_computation.1 | async-start | bytes 4194304 | tf_op jit(solution)/shard_map/all_to_all | solution.py:58
  213.4 4.3 %fusion.18 = f32[1,1024]{1,0:T(1,128)S(1)} fusion(f32[1024,1]{0,1:T(1,128)S(1)} %bitcast.59, f32[1024,1024]{1,0:T(8,128)} %copy-done), kind=kOutput, calls=%fused_computation.40 | convolution fusion | flops 12582912 | bytes 4202496 | tf_op jit(solution)/shard_map/dot_general | solution.py:36
  217.6 78.1 %psum.51 = f32[1024]{0:T(1024)S(1)} all-reduce(f32[1024]{0:T(1024)S(1)} %bitcast.63), channel_id=1, replica_groups=mesh['cent'=8,'dp'=32] {'dp'}, use_global_device_ids=true, to_apply=%region_4.0 | all-reduce | flops 1024 | bytes 8192 | tf_op jit(solution)/shard_map/psum | solution.py:37
  295.7 5.8 %fusion.19 = f32[1,1024]{1,0:T(1,128)S(1)} fusion(f32[1024,1024]{1,0:T(8,128)} %copy-done, f32[1024,1]{0,1:T(1,128)S(1)} %bitcast.64), kind=kOutput, calls=%fused_computation.41 | convolution fusion | flops 12582912 | bytes 4202496 | tf_op jit(solution)/shard_map/dot_general | solution.py:38
  301.5 14.2 %psum.52 = f32[1024]{0:T(1024)S(1)} all-reduce(f32[1024]{0:T(1024)S(1)} %bitcast.65), channel_id=1, replica_groups=mesh['cent'=8,'dp'=32] {'cent'}, use_global_device_ids=true, to_apply=%region_5.0 | all-reduce | flops 1024 | bytes 8192 | tf_op jit(solution)/shard_map/psum | solution.py:40
  315.7 4.3 %fusion.20 = f32[1,1024]{1,0:T(1,128)S(1)} fusion(f32[1024,1]{0,1:T(1,128)S(1)} %bitcast.66, f32[1024,1024]{1,0:T(8,128)} %copy-done), kind=kOutput, calls=%fused_computation.42 | convolution fusion | flops 12582912 | bytes 4202496 | tf_op jit(solution)/shard_map/dot_general | solution.py:36
  319.9 62.7 %psum.53 = f32[1024]{0:T(1024)S(1)} all-reduce(f32[1024]{0:T(1024)S(1)} %bitcast.67), channel_id=1, replica_groups=mesh['cent'=8,'dp'=32] {'dp'}, use_global_device_ids=true, to_apply=%region_6.0 | all-reduce | flops 1024 | bytes 8192 | tf_op jit(solution)/shard_map/psum | solution.py:37
  382.6 5.8 %fusion.21 = f32[1,1024]{1,0:T(1,128)S(1)} fusion(f32[1024,1024]{1,0:T(8,128)} %copy-done, f32[1024,1]{0,1:T(1,128)S(1)} %bitcast.54), kind=kOutput, calls=%fused_computation.43 | convolution fusion | flops 12582912 | bytes 4202496 | tf_op jit(solution)/shard_map/dot_general | solution.py:38
  388.4 0.0 all-to-all-done.1
  388.4 2.8 gather_fusion
  391.2 0.2 reduce_sum.59
  391.4 16.5 %all-reduce = (f32[1024]{0:T(1024)S(1)}, f32[1024]{0:T(1024)S(1)}) all-reduce(f32[1024]{0:T(1024)S(1)} %bitcast.60, f32[1024]{0:T(1024)S(1)} %reduce_sum.59), channel_id=1, replica_groups=mesh['cent'=8,'dp'=32] {'cent'}, use_global_device_ids=true, to_apply=%region_7.0 | all-reduce | flops 2048 | bytes 16384 | tf_op jit(solution)/shard_map/psum | solution.py:62
  407.9 4.0 multiply_convert_fusion
  412.0 0.9 divide_convert_fusion
  (13 shorter events, 0.1 us)
Async XLA Ops:
  13.5 8.3 %copy-start.1 = (bf16[1024,1024]{1,0:T(8,128)(2,1)S(1)}, bf16[1024,1024]{1,0:T(8,128)(2,1)}, u32[]{:S(2)}) copy-start(bf16[1024,1024]{1,0:T(8,128)(2,1)} %param.4) | copy-start | bytes 6291460
  13.5 183.0 %all-to-all-start = ((bf16[32,128,1024]{2,1,0:T(8,128)(2,1)}), bf16[32,128,1024]{2,1,0:T(8,128)(2,1)}, u32[]{:S(2)}, u32[]{:S(2)}) async-start(bf16[32,128,1024]{2,1,0:T(8,128)(2,1)} %bitcast.51), calls=%async_computation | async-start | bytes 16777216 | tf_op jit(solution)/shard_map/all_to_all | solution.py:52
  19.6 2.7 copy-start.2
  24.9 1.9 copy-start
  26.9 169.4 %copy-start.3 = (bf16[2,128,1024]{2,1,0:T(8,128)(2,1)S(1)}, bf16[2,128,1024]{2,1,0:T(8,128)(2,1)}, u32[]{:S(2)}) copy-start(bf16[2,128,1024]{2,1,0:T(8,128)(2,1)} %param.7) | copy-start | bytes 1572868
  208.0 180.4 %all-to-all-start.1 = ((f32[32,128,128]{2,1,0:T(8,128)}), f32[32,128,128]{2,1,0:T(8,128)S(1)}, u32[]{:S(2)}, u32[]{:S(2)}) async-start(f32[32,128,128]{2,1,0:T(8,128)} %bitcast.53), calls=%async_computation.1 | async-start | bytes 4194304 | tf_op jit(solution)/shard_map/all_to_all | solution.py:58
where the time goes:
time: 414 us; the launch traced here: 413 us
  blocking collectives  333 us (80%)
  matrix products  36.6 us (9%)
  local copies, waits for them, and re-layouts  17.1 us (4%)
  other arithmetic  13.9 us (3%)
  starting transfers between devices  11.5 us (3%)
    psum x3, blocking collectives, shards(): col_scale = 1.0 / lax.psum(col_part, 'dp')  282 us
    psum x2, blocking collectives, shards(): row_scale = 1.0 / lax.psum(row_part, 'cent')  34.2 us
    dot_general x3, matrix products, shards(): row_part = jnp.dot(expo, col_scale, precision=lax.Precision.HIGHEST)  17.3 us
    psum x1, blocking collectives, shards(): row_total = lax.psum(row_part, 'cent')  16.5 us
    scatter x1, local copies, waits for them, and re-layouts, shards(): jnp.zeros((clusters * CAP, width), jnp.bfloat16).at[slot].set(points)  10.8 us
    dot_general x3, matrix products, shards(): col_part = jnp.dot(row_scale, expo, precision=lax.Precision.HIGHEST)  10.6 us
  transfers between devices with their start and end apart: 2, of which 0 were waited for; matrix products, arithmetic and copies ran while one was open for 8% of the time, Pallas kernels for 0%

commit v1 on v0

--- a/solution.py
+++ b/solution.py
@@ -59,7 +59,11 @@
     slot_weights = returned.reshape(clusters * CAP, sub_dev)
     point_weights = slot_weights[slot]
     denom_part = jnp.sum(point_weights, axis=1)
-    row_total = lax.psum(row_part, "cent")
+    row_total = row_part
+    for hop in (1, 2, 4):
+        row_total = row_total + lax.ppermute(
+            row_total, "cent", [(dev, dev ^ hop) for dev in range(8)]
+        )
     denominator = lax.psum(denom_part, "cent")
     row_scale = 1.0 / row_total
     assign = (expo * row_scale[:, None] * col_scale[None, :] * total_cent).astype(jnp.bfloat16)

time: 414 us -> 455 us (1.099)
  waiting for transfers between devices: 0.01 us -> 115 us
  blocking collectives: 333 us -> 238 us
  starting transfers between devices: 11.5 us -> 30.3 us
    all_to_all x1, waiting for transfers between devices: 0.01 us -> 106 us  [shards(): lax.all_to_all(outgoing, 'dp', split_axis=0, concat_axis=0, tiled=True)]
    psum x3, blocking collectives: 282 us -> 204 us  [shards(): col_scale = 1.0 / lax.psum(col_part, 'dp')]
    psum x1 -> x0, blocking collectives: 16.5 us -> none  [shards(): row_total = lax.psum(row_part, 'cent')]
    all_to_all x1, starting transfers between devices: 5.4 us -> 18.4 us  [shards(): lax.all_to_all(weights, 'dp', split_axis=0, concat_axis=0, tiled=True)]
    ppermute x0 -> x3, waiting for transfers between devices: none -> 9.11 us  [shards(): lax.ppermute(row_total, 'cent', [(dev, dev ^ hop) for dev in range(8)])]
    ppermute x0 -> x3, starting transfers between devices: none -> 5.65 us  [shards(): lax.ppermute(row_total, 'cent', [(dev, dev ^ hop) for dev in range(8)])]
  transfers between devices with their start and end apart: 2 -> 5, of which waited for: 0 -> 4; matrix products, arithmetic and copies ran while one was open for 8% -> 6% of each run, Pallas kernels for 0% -> 0%
where the time goes in v1:
time: 455 us; the launch traced here: 452 us
  blocking collectives  238 us (52%)
  waiting for transfers between devices  115 us (25%)
  matrix products  40.8 us (9%)
  starting transfers between devices  30.3 us (7%)
  local copies, waits for them, and re-layouts  15.2 us (3%)
  other arithmetic  11.7 us (3%)
    psum x3, blocking collectives, shards(): col_scale = 1.0 / lax.psum(col_part, 'dp')  204 us
    all_to_all x1, waiting for transfers between devices, shards(): lax.all_to_all(outgoing, 'dp', split_axis=0, concat_axis=0, tiled=True)  106 us
    psum x2, blocking collectives, shards(): row_scale = 1.0 / lax.psum(row_part, 'cent')  34.6 us
    all_to_all x1, starting transfers between devices, shards(): lax.all_to_all(weights, 'dp', split_axis=0, concat_axis=0, tiled=True)  18.4 us
    dot_general x3, matrix products, shards(): row_part = jnp.dot(expo, col_scale, precision=lax.Precision.HIGHEST)  17.4 us
    dot_general x3, matrix products, shards(): col_part = jnp.dot(row_scale, expo, precision=lax.Precision.HIGHEST)  12.8 us
    scatter x1, local copies, waits for them, and re-layouts, shards(): jnp.zeros((clusters * CAP, width), jnp.bfloat16).at[slot].set(points)  10.8 us
    ppermute x3, waiting for transfers between devices, shards(): lax.ppermute(row_total, 'cent', [(dev, dev ^ hop) for dev in range(8)])  9.11 us
  transfers between devices with their start and end apart: 5, of which 4 were waited for; matrix products, arithmetic and copies ran while one was open for 6% of the time, Pallas kernels for 0%

profile of v1, /device:TPU:0, one launch (start us, length us, event | category | flops | bytes accessed | tf_op | source)
XLA Modules:
  0.0 452.2 jit_solution(3247256039367937655)
XLA Ops:
  0.6 1.4 fusion.11
  2.0 0.7 compare_select_fusion
  2.7 10.8 %scatter_custom_fusion = bf16[4096,1024]{1,0:T(8,128)(2,1)} fusion(s32[1024]{0:T(1024)S(1)} %bitcast.56, bf16[1024,1024]{1,0:T(8,128)(2,1)} %param.4, bf16[]{:T(256)} %constant.6.clone.1), kind=kCustom, calls=%fused_computation.6 | custom fusion | bytes 8389120 | tf_op jit(solution)/shard_map/scatter | solution.py:49
  13.5 0.0 copy-start.3
  13.5 0.0 copy-start.1
  13.5 6.2 %all-to-all-start = ((bf16[32,128,1024]{2,1,0:T(8,128)(2,1)}), bf16[32,128,1024]{2,1,0:T(8,128)(2,1)}, u32[]{:S(2)}, u32[]{:S(2)}) async-start(bf16[32,128,1024]{2,1,0:T(8,128)(2,1)} %bitcast.51), calls=%async_computation | async-start | bytes 16777216 | tf_op jit(solution)/shard_map/all_to_all | solution.py:52
  19.7 0.0 copy-done.3
  19.7 0.0 copy-start.2
  19.7 0.2 multiply_reduce_fusion.3
  19.9 2.2 multiply_reduce_fusion.1
  22.1 0.0 copy-done.1
  22.1 0.5 multiply_reduce_fusion.2
  22.6 0.0 copy-done.2
  22.6 4.5 multiply_exponential_fusion
  27.1 106.1 %all-to-all-done = bf16[32,128,1024]{2,1,0:T(8,128)(2,1)} async-done(((bf16[32,128,1024]{2,1,0:T(8,128)(2,1)}), bf16[32,128,1024]{2,1,0:T(8,128)(2,1)}, u32[]{:S(2)}, u32[]{:S(2)}) %all-to-all-start) | async-done | bytes 8388640 | tf_op jit(solution)/shard_map/all_to_all | solution.py:52
  133.2 5.1 %multiply_reduce_fusion = f32[32,128]{1,0:T(8,128)S(1)} fusion(bf16[32,128,1024]{2,1,0:T(8,128)(2,1)} %all-to-all-done), kind=kLoop, calls=%fused_computation.2 | loop fusion | flops 12578816 | bytes 8404992 | tf_op jit(solution)/shard_map/reduce_sum | solution.py:14
  138.3 0.1 rsqrt.34
  138.4 4.8 %fusion.7 = f32[32,2,64,128]{3,2,0,1:T(8,128)S(1)} fusion(bf16[32,2,64,1024]{3,2,1,0:T(8,128)(2,1)} %bitcast.16, f32[2,128]{1,0:T(2,128)S(1)} %add_rsqrt_fusion.3, f32[32,2,64]{2,0,1:T(8,128)S(1)} %copy.7, bf16[2,128,1024]{2,1,0:T(8,128)(2,1)S(1)} %copy-done.3), kind=kOutput, calls=%fused_computation.16 | convolution fusion | flops 1075314688 | bytes 11027456 | tf_op jit(solution)/shard_map/sgcd,gkd->sgck/dot_general | solution.py:55
  143.2 1.5 copy.8
  144.7 18.4 %all-to-all-start.1 = ((f32[32,128,128]{2,1,0:T(8,128)}), f32[32,128,128]{2,1,0:T(8,128)S(1)}, u32[]{:S(2)}, u32[]{:S(2)}) async-start(f32[32,128,128]{2,1,0:T(8,128)} %bitcast.53), calls=%async_computation.1 | async-start | bytes 4194304 | tf_op jit(solution)/shard_map/all_to_all | solution.py:58
  163.1 4.3 fusion.14
  167.4 78.3 %psum.42 = f32[1024]{0:T(1024)S(1)} all-reduce(f32[1024]{0:T(1024)S(1)} %bitcast.55), channel_id=1, replica_groups=mesh['cent'=8,'dp'=32] {'dp'}, use_global_device_ids=true, to_apply=%region_2.0 | all-reduce | flops 1024 | bytes 8192 | tf_op jit(solution)/shard_map/psum | solution.py:37
  245.7 5.8 %fusion.17 = f32[1,1024]{1,0:T(1,128)S(1)} fusion(f32[1024,1024]{1,0:T(8,128)} %multiply_exponential_fusion, f32[1024,1]{0,1:T(1,128)S(1)} %bitcast.62), kind=kOutput, calls=%fused_computation.39 | convolution fusion | flops 12582912 | bytes 4202496 | tf_op jit(solution)/shard_map/dot_general | solution.py:38
  251.4 20.2 %psum.43 = f32[1024]{0:T(1024)S(1)} all-reduce(f32[1024]{0:T(1024)S(1)} %bitcast.63), channel_id=1, replica_groups=mesh['cent'=8,'dp'=32] {'cent'}, use_global_device_ids=true, to_apply=%region_3.0 | all-reduce | flops 1024 | bytes 8192 | tf_op jit(solution)/shard_map/psum | solution.py:40
  271.7 4.3 fusion.18
  275.9 62.7 %psum.44 = f32[1024]{0:T(1024)S(1)} all-reduce(f32[1024]{0:T(1024)S(1)} %bitcast.65), channel_id=1, replica_groups=mesh['cent'=8,'dp'=32] {'dp'}, use_global_device_ids=true, to_apply=%region_4.0 | all-reduce | flops 1024 | bytes 8192 | tf_op jit(solution)/shard_map/psum | solution.py:37
  338.6 5.8 %fusion.19 = f32[1,1024]{1,0:T(1,128)S(1)} fusion(f32[1024,1024]{1,0:T(8,128)} %multiply_exponential_fusion, f32[1024,1]{0,1:T(1,128)S(1)} %bitcast.66), kind=kOutput, calls=%fused_computation.41 | convolution fusion | flops 12582912 | bytes 4202496 | tf_op jit(solution)/shard_map/dot_general | solution.py:38
  344.4 0.0 all-to-all-done.1
  344.4 2.8 gather_fusion
  347.2 0.2 reduce_sum.59
  347.4 14.4 %all-reduce = (f32[1024]{0:T(1024)S(1)}, f32[1024]{0:T(1024)S(1)}) all-reduce(f32[1024]{0:T(1024)S(1)} %bitcast.61, f32[1024]{0:T(1024)S(1)} %reduce_sum.59), channel_id=1, replica_groups=mesh['cent'=8,'dp'=32] {'cent'}, use_global_device_ids=true, to_apply=%region_5.0 | all-reduce | flops 2048 | bytes 16384 | tf_op jit(solution)/shard_map/psum | solution.py:40
  361.9 4.3 fusion.20
  366.1 62.7 %psum.46 = f32[1024]{0:T(1024)S(1)} all-reduce(f32[1024]{0:T(1024)S(1)} %bitcast.68), channel_id=1, replica_groups=mesh['cent'=8,'dp'=32] {'dp'}, use_global_device_ids=true, to_apply=%region_6.0 | all-reduce | flops 1024 | bytes 8192 | tf_op jit(solution)/shard_map/psum | solution.py:37
  428.8 0.0 copy-start
  428.8 5.9 %fusion.21 = f32[1,1024]{1,0:T(1,128)S(1)} fusion(f32[1024,1024]{1,0:T(8,128)} %multiply_exponential_fusion, f32[1024,1]{0,1:T(1,128)S(1)} %bitcast.54), kind=kOutput, calls=%fused_computation.43 | convolution fusion | flops 12582912 | bytes 4202496 | tf_op jit(solution)/shard_map/dot_general | solution.py:38
  434.7 2.1 collective-permute-start
  436.8 1.6 collective-permute-done
  438.3 0.2 collective-permute-start.1
  438.6 4.3 collective-permute-done.1
  442.9 3.3 collective-permute-start.2
  446.2 0.9 divide_convert_fusion
  447.1 3.3 collective-permute-done.2
  450.4 0.0 copy-done
  450.4 1.9 multiply_convert_fusion
  (15 shorter events, 0.1 us)
Async XLA Ops:
  13.5 6.2 %copy-start.3 = (bf16[2,128,1024]{2,1,0:T(8,128)(2,1)S(1)}, bf16[2,128,1024]{2,1,0:T(8,128)(2,1)}, u32[]{:S(2)}) copy-start(bf16[2,128,1024]{2,1,0:T(8,128)(2,1)} %param.7) | copy-start | bytes 1572868
  13.5 8.6 %copy-start.1 = (bf16[1024,1024]{1,0:T(8,128)(2,1)S(1)}, bf16[1024,1024]{1,0:T(8,128)(2,1)}, u32[]{:S(2)}) copy-start(bf16[1024,1024]{1,0:T(8,128)(2,1)} %param.4) | copy-start | bytes 6291460
  13.5 119.7 %all-to-all-start = ((bf16[32,128,1024]{2,1,0:T(8,128)(2,1)}), bf16[32,128,1024]{2,1,0:T(8,128)(2,1)}, u32[]{:S(2)}, u32[]{:S(2)}) async-start(bf16[32,128,1024]{2,1,0:T(8,128)(2,1)} %bitcast.51), calls=%async_computation | async-start | bytes 16777216 | tf_op jit(solution)/shard_map/all_to_all | solution.py:52
  19.7 2.9 copy-start.2
  144.7 199.7 %all-to-all-start.1 = ((f32[32,128,128]{2,1,0:T(8,128)}), f32[32,128,128]{2,1,0:T(8,128)S(1)}, u32[]{:S(2)}, u32[]{:S(2)}) async-start(f32[32,128,128]{2,1,0:T(8,128)} %bitcast.53), calls=%async_computation.1 | async-start | bytes 4194304 | tf_op jit(solution)/shard_map/all_to_all | solution.py:58
  428.8 21.6 %copy-start = (f32[1024,1024]{1,0:T(8,128)S(1)}, f32[1024,1024]{1,0:T(8,128)}, u32[]{:S(2)}) copy-start(f32[1024,1024]{1,0:T(8,128)} %multiply_exponential_fusion) | copy-start | bytes 12582916
  434.7 3.6 collective-permute-start
  438.3 4.5 collective-permute-start.1
  442.9 7.5 %collective-permute-start.2 = (f32[1024]{0:T(1024)S(1)}, f32[1024]{0:T(1024)S(1)}, u32[]{:S(2)}, u32[]{:S(2)}) collective-permute-start(f32[1024]{0:T(1024)S(1)} %add.68), channel_id=1, source_target_pairs={{0,128},{32,160},{64,192},{96,224},{128,0},{160,32},{192,64},{224,... | collective-permute-start | bytes 12296 | tf_op jit(solution)/shard_map/ppermute | solution.py:64
